TPU v7x, 128 devices: a whole 4x4x4 slice. The times are simulated.
128 devices in a mesh: req: 16 (over y, x), kvh: 8 (over z, core).
Axes of the slice: x: 4, y: 4, z: 4, core: 2. Of those that a mesh axis runs over, the one named last changes fastest.
Arguments:
- states: bfloat16 [128, 2560], P('req', 'kvh'), may hold values from -6 to 6
- attn_gain: bfloat16 [2560], replicated, may hold values from 0.099609375 to 1.8984375
- w_query: bfloat16 [2560, 4096], P(None, 'kvh'), may hold values from -0.125 to 0.125
- w_key: bfloat16 [2560, 1024], P(None, 'kvh'), may hold values from -0.125 to 0.125
- w_value: bfloat16 [2560, 1024], P(None, 'kvh'), may hold values from -0.125 to 0.125
- query_gain: bfloat16 [128], replicated, may hold values from 0.5 to 2
- key_gain: bfloat16 [128], replicated, may hold values from 0.5 to 2
- w_output: bfloat16 [4096, 2560], P('kvh'), may hold values from -0.25 to 0.25
- ffn_gain: bfloat16 [2560], P('kvh'), may hold values from 0.099609375 to 1.8984375
- w_gate: bfloat16 [2560, 9728], P('kvh', 'req'), may hold values from -0.125 to 0.125
- w_up: bfloat16 [2560, 9728], P('kvh', 'req'), may hold values from -0.125 to 0.125
- w_down: bfloat16 [9728, 2560], P('req', 'kvh'), may hold values from -0.0625 to 0.0625
- kv_pool: bfloat16 [1024, 8, 128, 256], P('req', 'kvh'), may hold values from -6 to 6
- lengths: int32 [128], replicated, may hold values from 1 to 1023, as said below
- page_table: int32 [128, 8], P('req'), may hold values from 0 to 63, as said below
- new_order: int32 [128], replicated, may hold values from 0 to 127, as said below
Outputs:
- output: bfloat16 [128, 2560], P('req', 'kvh')
- new_pool: bfloat16 [1024, 8, 128, 256], P('req', 'kvh')
Inputs may be any that keep to these rules, and one draw needn't show every extreme that they name: `lengths`: each request has at least one cached position and room for the new one; some request has exactly 1023. `page_table`: the 8 rows of one device name each of its 64 pool rows exactly once. `new_order`: A permutation of the requests; slot s lies on the device s // 8. The 8 requests of one device go to 8 different devices, and each device receives its 8 requests from 8 different devices.
All inputs are finite; a program needn't handle non-finite values.
Results may differ from a plain program's by a relative error of at most 0.0087.
Values may be sent and summed in bfloat16 or wider, within the bound.
No kernel may reach another device: no remote copies, remote signals or barrier semaphores. Data moves between devices by JAX's collectives and lax.ppermute only.
A program may use at most 128 MiB of HBM per device.

v0:
```python
import math
import jax
import jax.numpy as jnp
from jax import lax
from jax.sharding import PartitionSpec as P

D = 2560
EPSILON = 1e-06


def rms_norm(values, norm_gain):
    mean_sq = jnp.mean(values * values, axis=-1, keepdims=True)
    return values * lax.rsqrt(mean_sq + EPSILON) * norm_gain


def rotary(values, positions):
    half_dim = values.shape[-1] // 2
    frequency = jnp.exp(
        jnp.arange(half_dim, dtype=jnp.float32) * (-2.0 * math.log(1000000.0) / values.shape[-1])
    )
    angles = positions.astype(jnp.float32)[:, None, None] * frequency
    cosine = jnp.cos(angles)
    sine_part = jnp.sin(angles)
    first_half = values[..., :half_dim]
    second_half = values[..., half_dim:]
    return jnp.concatenate(
        [
            first_half * cosine - second_half * sine_part,
            second_half * cosine + first_half * sine_part,
        ],
        axis=-1,
    )


def mask_blocks(blocks, lengths_now, fresh):
    row_count, pages_per, kv_local, page_len, channels = blocks.shape
    positions = (
        jnp.arange(pages_per, dtype=jnp.int32)[:, None] * page_len
        + jnp.arange(page_len, dtype=jnp.int32)[None, :]
    )
    positions = positions[None, :, None, :, None]
    lengths_col = lengths_now[:, None, None, None, None]
    kept = positions < lengths_col
    placed = positions == lengths_col
    return jnp.where(
        kept, blocks, jnp.where(placed, fresh[:, None, :, None, :], jnp.zeros((), jnp.bfloat16))
    )


def attend(query, sequence, lengths_now):
    row_count, kv_local, span_len, channels = sequence.shape
    head_dim = channels // 2
    q_local = query.shape[1]
    group_size = q_local // kv_local
    grouped = query.reshape(row_count, kv_local, group_size, head_dim)
    scores = jnp.einsum(
        "rkgd,rktd->rkgt", grouped, sequence[..., :head_dim], preferred_element_type=jnp.float32
    ) * (1.0 / math.sqrt(head_dim))
    positions = jnp.arange(span_len, dtype=jnp.int32)
    valid = positions[None, None, None, :] <= lengths_now[:, None, None, None]
    scores = jnp.where(valid, scores, -jnp.inf)
    weights = jax.nn.softmax(scores, axis=-1).astype(jnp.bfloat16)
    mixed = jnp.einsum(
        "rkgt,rktd->rkgd", weights, sequence[..., head_dim:], preferred_element_type=jnp.float32
    )
    return mixed.reshape(row_count, q_local * head_dim).astype(jnp.bfloat16)


def per_device(
    states,
    attn_gain,
    w_query,
    w_key,
    w_value,
    query_gain,
    key_gain,
    w_output,
    ffn_gain,
    w_gate,
    w_up,
    w_down,
    kv_pool,
    lengths,
    page_table,
    new_order,
):
    devices_req = lax.axis_size("req")
    my_index = lax.axis_index("req")
    kvh_index = lax.axis_index("kvh")
    row_count = states.shape[0]
    width_local = states.shape[1]
    head_dim = query_gain.shape[0]
    kv_local = w_key.shape[1] // head_dim
    q_local = w_query.shape[1] // head_dim
    pages_per = page_table.shape[1]
    page_len = kv_pool.shape[2]
    channels = 2 * head_dim
    total_rows = new_order.shape[0]
    everyone = jnp.arange(total_rows, dtype=jnp.int32)
    new_position = jnp.zeros((total_rows,), jnp.int32).at[new_order].set(everyone)
    home = my_index * row_count + jnp.arange(row_count, dtype=jnp.int32)
    destination = new_position[home] // row_count
    peer_ids = jnp.arange(devices_req, dtype=jnp.int32)
    matches = destination[None, :] == peer_ids[:, None]
    picked = jnp.argmax(matches.astype(jnp.int32), axis=1)
    parcels = kv_pool[page_table[picked]]
    received = lax.all_to_all(parcels, "req", split_axis=0, concat_axis=0, tiled=True)
    arriving = lax.dynamic_slice_in_dim(new_order, my_index * row_count, row_count)
    source_owner = arriving // row_count
    full_states = lax.all_gather(states, "kvh", axis=1, tiled=True)
    normed = rms_norm(full_states.astype(jnp.float32), attn_gain.astype(jnp.float32)).astype(
        jnp.bfloat16
    )
    query = jnp.dot(normed, w_query, preferred_element_type=jnp.float32).reshape(
        row_count, q_local, head_dim
    )
    key_new = jnp.dot(normed, w_key, preferred_element_type=jnp.float32).reshape(
        row_count, kv_local, head_dim
    )
    value_new = jnp.dot(normed, w_value, preferred_element_type=jnp.float32).reshape(
        row_count, kv_local, head_dim
    )
    positions_home = lengths[home]
    query = rotary(rms_norm(query, query_gain.astype(jnp.float32)), positions_home).astype(
        jnp.bfloat16
    )
    key_new = rotary(rms_norm(key_new, key_gain.astype(jnp.float32)), positions_home).astype(
        jnp.bfloat16
    )
    fresh = jnp.concatenate([key_new, value_new.astype(jnp.bfloat16)], axis=-1)
    home_blocks = mask_blocks(kv_pool[page_table], positions_home, fresh)
    sequence = home_blocks.transpose(0, 2, 1, 3, 4).reshape(
        row_count, kv_local, pages_per * page_len, channels
    )
    mixed = attend(query, sequence, positions_home)
    partial_out = jnp.dot(mixed, w_output, preferred_element_type=jnp.float32)
    attn_out = lax.psum(partial_out, "kvh")
    residual_full = (full_states.astype(jnp.float32) + attn_out).astype(jnp.bfloat16)
    residual_wide_full = residual_full.astype(jnp.float32)
    total_sq = jnp.sum(residual_wide_full * residual_wide_full, axis=-1, keepdims=True)
    residual_wide = lax.dynamic_slice_in_dim(
        residual_wide_full, kvh_index * width_local, width_local, axis=1
    )
    normed_two = (
        residual_wide * lax.rsqrt(total_sq / D + EPSILON) * ffn_gain.astype(jnp.float32)
    ).astype(jnp.bfloat16)
    fresh_flat = fresh.reshape(row_count, kv_local * channels)
    gathered = lax.all_gather(
        jnp.concatenate([normed_two, fresh_flat], axis=1), "req", axis=0, tiled=True
    )
    normed_all = gathered[:, :width_local]
    fresh_all = gathered[:, width_local:].reshape(total_rows, kv_local, channels)
    ffn_width = w_gate.shape[1]
    joined = jnp.concatenate([w_gate, w_up], axis=1)
    partial_both = jnp.dot(normed_all, joined, preferred_element_type=jnp.float32)
    summed = lax.psum(partial_both, "kvh")
    hidden = (jax.nn.silu(summed[:, :ffn_width]) * summed[:, ffn_width:]).astype(jnp.bfloat16)
    lowered = lax.psum_scatter(
        jnp.dot(hidden, w_down, preferred_element_type=jnp.float32),
        "req",
        scatter_dimension=0,
        tiled=True,
    )
    result = (residual_wide + lowered).astype(jnp.bfloat16)
    arrived = received[source_owner]
    new_blocks = mask_blocks(arrived, lengths[arriving], fresh_all[arriving])
    new_pool = new_blocks.reshape(row_count * pages_per, kv_local, page_len, channels)
    return (result, new_pool)


def solution(mesh):
    in_specs = (
        P("req", "kvh"),
        P(),
        P(None, "kvh"),
        P(None, "kvh"),
        P(None, "kvh"),
        P(),
        P(),
        P("kvh", None),
        P("kvh"),
        P("kvh", "req"),
        P("kvh", "req"),
        P("req", "kvh"),
        P("req", "kvh", None, None),
        P(),
        P("req", None),
        P(),
    )
    out_specs = (P("req", "kvh"), P("req", "kvh", None, None))
    return jax.shard_map(
        per_device, mesh=mesh, in_specs=in_specs, out_specs=out_specs, check_vma=False
    )
```

profile of v0, /device:TPU:0, one launch (start us, length us, event | category | flops | bytes accessed | tf_op | source)
XLA Modules:
  0.0 340.9 jit_solution(16654045882225741350)
XLA Ops:
  7.2 0.8 compare_select_fusion.4
  8.0 1.0 scatter_custom_fusion
  9.0 0.6 gather_fusion.3
  9.7 0.6 iota_reduce_fusion
  10.3 1.2 gather_fusion.4
  11.7 0.1 reshape.467
  11.8 8.7 %gather_fusion.5 = bf16[128,128,256]{2,1,0:T(8,128)(2,1)} fusion(bf16[64,128,256]{2,1,0:T(8,128)(2,1)} %bitcast.79, s32[1024]{0:T(1024)S(1)} %pad_clamp_fusion.1), kind=kCustom, calls=%fused_computation.5 | custom fusion | bytes 16777728 | tf_op jit(solution)/shard_map/gather | solution.py:106
  20.5 7.3 %all-to-all-start = ((bf16[16,8,1,128,256]{4,3,1,2,0:T(8,128)(2,1)}), bf16[16,8,1,128,256]{4,3,1,2,0:T(8,128)(2,1)}, u32[]{:S(2)}, u32[]{:S(2)}) async-start(bf16[16,8,1,128,256]{4,3,1,2,0:T(8,128)(2,1)} %bitcast.81), calls=%async_computation | async-start | bytes 16777216 | tf_op jit(solution)/shard_map/all_to_all | solution.py:107
  27.9 0.6 gather_fusion
  28.6 0.1 reshape.433
  28.7 14.0 %all-gather = bf16[8,320,8]{1,2,0:T(8,128)(2,1)S(1)} all-gather(bf16[1,320,8]{1,2,0:T(8,128)(2,1)S(1)} %bitcast.84), channel_id=1, replica_groups=mesh['req'=16,'kvh'=8] {'kvh'}, dimensions={0}, use_global_device_ids=true | all-gather | bytes 46080 | tf_op jit(solution)/shard_map/all_gather | solution.py:110
  42.8 0.1 reshape.517
  42.9 0.1 fusion.18
  43.0 0.1 fusion.20
  43.1 2.3 multiply_reduce_fusion.1
  45.4 0.1 copy.33
  45.4 5.1 %gather_fusion.1 = bf16[64,128,256]{2,1,0:T(8,128)(2,1)} fusion(bf16[64,128,256]{2,1,0:T(8,128)(2,1)} %bitcast.80, s32[1024]{0:T(1024)S(1)} %pad_clamp_fusion.4), kind=kCustom, calls=%fused_computation.1 | custom fusion | bytes 8388864 | tf_op jit(solution)/shard_map/gather | solution.py:131
  50.6 0.2 fusion.9
  50.8 1.4 multiply_reduce_fusion.2
  52.3 0.1 fusion.37
  52.4 0.1 maximum_bitcast_fusion
  52.5 0.1 multiply_cosine_fusion.1
  52.7 0.1 broadcast_compare_fusion.1
  52.7 0.1 fusion.24
  52.8 0.1 subtract_convert_fusion
  52.9 7.6 %select_select_fusion.1 = bf16[8,1,1024,256]{3,2,0,1:T(8,128)(2,1)} fusion(bf16[8,1,1024,256]{3,2,0,1:T(8,128)(2,1)} %bitcast.83, pred[8,1024]{1,0:T(8,128)(4,1)S(1)} %get-tuple-element.13, pred[8,1024]{1,0:T(8,128)(4,1)S(1)} %get-tuple-element.12, bf16[8,256]{1,0:T(8,128)(2,1)S(1)} %maximum_bitcast_fusion), kind=kLoop, calls=%fused_computation.11 | loop fusion | flops 4194304 | bytes 8409088 | tf_op jit(solution)/shard_map/jit(_where)/select_n | solution.py:45
  60.6 2.5 fusion.48
  63.1 2.0 fusion.8
  65.1 1.1 fusion.26
  66.3 0.1 compare_select_fusion.9
  66.4 0.6 gather_fusion.2
  67.1 0.1 lt.108
  67.2 0.6 dynamic-slice
  68.5 56.2 %all-reduce.5.cloned.1.call-done = f32[8,2560]{1,0:T(8,128)} async-done(((f32[8,2560]{1,0:T(8,128)}), f32[8,2560]{1,0:T(8,128)}) %all-reduce.5.cloned.1.call-update) | async-done | bytes 81936 | tf_op jit(solution)/shard_map/psum | solution.py:137
  124.7 1.0 multiply_reduce_fusion
  125.7 0.1 multiply_convert_fusion
  125.8 0.1 pad_maximum_fusion
  125.9 41.0 %all_gather.7 = bf16[128,576]{1,0:T(8,128)(2,1)S(1)} all-gather(bf16[8,576]{1,0:T(8,128)(2,1)S(1)} %pad_maximum_fusion), channel_id=1, replica_groups=mesh['req'=16,'kvh'=8] {'req'}, dimensions={0}, use_global_device_ids=true | all-gather | bytes 156672 | tf_op jit(solution)/shard_map/all_gather | solution.py:148
  166.9 2.7 fusion.10
  169.7 0.1 bitcast_compare_fusion.1
  169.7 0.1 slice.63
  169.8 0.6 gather_fusion.7
  170.4 62.3 %all-reduce.7.cloned.1.call-done = f32[128,1216]{0,1:T(8,128)} async-done(((f32[128,1216]{0,1:T(8,128)}), f32[128,1216]{0,1:T(8,128)}) %all-reduce.7.cloned.1.call-update) | async-done | bytes 622608 | tf_op jit(solution)/shard_map/psum | solution.py:156
  232.8 2.2 fusion.15
  235.0 84.2 %all-reduce.9.cloned.1.call-done = f32[128,320]{1,0:T(8,128)} async-done(((f32[128,320]{1,0:T(8,128)}), f32[128,320]{1,0:T(8,128)}) %all-reduce.9.cloned.1.call-update) | async-done | bytes 163856
  319.2 1.4 fusion.25
  320.5 6.2 %gather_fusion.6 = bf16[8,8,128,256]{3,2,1,0:T(8,128)(2,1)} fusion(bf16[16,8,128,256]{3,2,1,0:T(8,128)(2,1)} %bitcast.16, s32[1024]{0:T(1024)S(1)} %pad_clamp_fusion), kind=kCustom, calls=%fused_computation.6 | custom fusion | bytes 8388640 | tf_op jit(solution)/shard_map/gather | solution.py:165
  326.7 7.6 %select_select_fusion = bf16[64,1,128,256]{3,2,1,0:T(8,128)(2,1)} fusion(bf16[64,1,128,256]{3,2,1,0:T(8,128)(2,1)} %bitcast.82, pred[64,128]{1,0:T(8,128)(4,1)S(1)} %get-tuple-element.11, pred[64,128]{1,0:T(8,128)(4,1)S(1)} %get-tuple-element.10, bf16[64,256]{1,0:T(8,128)(2,1)S(1)} %broadcast_bitcast_fusion), kind=kLoop, calls=%fused_computation.10 | loop fusion | flops 4194304 | bytes 8437760 | tf_op jit(solution)/shard_map/jit(_where)/select_n | solution.py:45
  (61 shorter events, 0.7 us)
Async XLA Ops:
  7.2 57.9 %copy-start = (bf16[512,2560]{1,0:T(8,128)(2,1)S(1)}, bf16[512,2560]{1,0:T(8,128)(2,1)}, u32[]{:S(2)}) copy-start(bf16[512,2560]{1,0:T(8,128)(2,1)} %param.23) | copy-start | bytes 7864324
  20.5 7.4 %copy-start.9 = (bf16[128]{0:T(256)(128)(2,1)S(1)}, bf16[128]{0:T(256)(128)(2,1)}, u32[]{:S(2)}) copy-start(bf16[128]{0:T(256)(128)(2,1)} %param.21) | copy-start | bytes 772
  20.5 7.5 %copy-start.10 = (bf16[128]{0:T(256)(128)(2,1)S(1)}, bf16[128]{0:T(256)(128)(2,1)}, u32[]{:S(2)}) copy-start(bf16[128]{0:T(256)(128)(2,1)} %param.22) | copy-start | bytes 772
  20.5 7.5 %copy-start.1 = (s32[128]{0:T(128)S(1)}, s32[128]{0:T(128)}, u32[]{:S(2)}) copy-start(s32[128]{0:T(128)} %param.29) | copy-start | bytes 1540
  20.5 8.1 %copy-start.2 = (s32[8,8]{1,0:T(8,128)S(1)}, s32[8,8]{1,0:T(8,128)}, u32[]{:S(2)}) copy-start(s32[8,8]{1,0:T(8,128)} %param.30) | copy-start | bytes 772
  20.5 8.2 %copy-start.5 = (bf16[2560]{0:T(1024)(128)(2,1)S(1)}, bf16[2560]{0:T(1024)(128)(2,1)}, u32[]{:S(2)}) copy-start(bf16[2560]{0:T(1024)(128)(2,1)} %param.17) | copy-start | bytes 15364
  20.5 8.2 %copy-start.4 = (bf16[8,320]{1,0:T(8,128)(2,1)S(1)}, bf16[8,320]{1,0:T(8,128)(2,1)}, u32[]{:S(2)}) copy-start(bf16[8,320]{1,0:T(8,128)(2,1)} %param.16) | copy-start | bytes 15364
  20.5 300.0 %all-to-all-start = ((bf16[16,8,1,128,256]{4,3,1,2,0:T(8,128)(2,1)}), bf16[16,8,1,128,256]{4,3,1,2,0:T(8,128)(2,1)}, u32[]{:S(2)}, u32[]{:S(2)}) async-start(bf16[16,8,1,128,256]{4,3,1,2,0:T(8,128)(2,1)} %bitcast.81), calls=%async_computation | async-start | bytes 16777216 | tf_op jit(solution)/shard_map/all_to_all | solution.py:107
  27.8 96.8 %all-reduce.5.cloned.1.call-start = ((), (), s32[]{:S(2)}) async-start(), calls=%async_computation.1 | async-start | bytes 163840 | tf_op jit(solution)/shard_map/psum | solution.py:137
  45.4 5.1 %copy-start.3 = (bf16[2560,128]{1,0:T(8,128)(2,1)S(1)}, bf16[2560,128]{1,0:T(8,128)(2,1)}, u32[]{:S(2)}) copy-start(bf16[2560,128]{1,0:T(8,128)(2,1)} %param.20) | copy-start | bytes 1966084
  60.5 5.7 %copy-start.7 = (s32[128]{0:T(128)S(1)}, s32[128]{0:T(128)}, u32[]{:S(2)}) copy-start(s32[128]{0:T(128)} %param.31) | copy-start | bytes 1540
  60.6 5.9 %copy-start.6 = (bf16[320]{0:T(512)(128)(2,1)S(1)}, bf16[320]{0:T(512)(128)(2,1)}, u32[]{:S(2)}) copy-start(bf16[320]{0:T(512)(128)(2,1)} %param.24) | copy-start | bytes 1924
  60.6 6.7 %copy-start.11 = (u32[128]{0:T(128)S(1)}, u32[128]{0:T(128)}, u32[]{:S(2)}) copy-start(u32[128]{0:T(128)} %constant.91) | copy-start | bytes 1540
  60.6 106.4 %copy-start.8 = (bf16[320,608]{1,0:T(8,128)(2,1)S(1)}, bf16[320,608]{1,0:T(8,128)(2,1)}, u32[]{:S(2)}) copy-start(bf16[320,608]{1,0:T(8,128)(2,1)} %param.26) | copy-start | bytes 1167364
  66.2 166.5 %all-reduce.7.cloned.1.call-start = ((), (), s32[]{:S(2)}) async-start(), calls=%async_computation.2 | async-start | bytes 1245184 | tf_op jit(solution)/shard_map/psum | solution.py:156
  169.6 149.6 %all-reduce.9.cloned.1.call-start = ((), (), s32[]{:S(2)}) async-start(), calls=%async_computation.3 | async-start | bytes 393216
Sparse Core Ops, SparseCore 0:
  66.4 58.2 all-reduce.4
  169.7 62.9 all-reduce.6
  236.5 82.5 all-reduce.8
where the time goes:
time: 342 us; the launch traced here: 341 us
  waiting for transfers between devices  203 us (59%)
  blocking collectives  55.1 us (16%)
  local copies, waits for them, and re-layouts  26.1 us (8%)
  other arithmetic  20.4 us (6%)
  between operations  14.7 us (4%)
  matrix products  14.3 us (4%)
  starting transfers between devices  7.46 us (2%)
    unnamed x4, waiting for transfers between devices  84.2 us
    psum x1, waiting for transfers between devices, per_device(): summed = lax.psum(partial_both, 'kvh')  62.3 us
    psum x1, waiting for transfers between devices, per_device(): attn_out = lax.psum(partial_out, 'kvh')  56.2 us
    all_gather x1, blocking collectives, per_device(): lax.all_gather(jnp.concatenate([normed_two, fresh_flat], axis=1), 'req',...  41 us
    select_n x2, other arithmetic, mask_blocks(): jnp.where(kept, blocks, jnp.where(placed, fresh[:, None, :, None, :], jnp...  15.3 us
    all_gather x1, blocking collectives, per_device(): full_states = lax.all_gather(states, 'kvh', axis=1, tiled=True)  14 us
    gather x3, local copies, waits for them, and re-layouts, per_device(): parcels = kv_pool[page_table[picked]]  9.99 us
    all_to_all x1, starting transfers between devices, per_device(): lax.all_to_all(parcels, 'req', split_axis=0, concat_axis=0, tiled=True)  7.34 us
  transfers between devices with their start and end apart: 4, of which 3 were waited for; matrix products, arithmetic and copies ran while one was open for 10% of the time, Pallas kernels for 0%

commit v1 on v0

--- a/solution.py
+++ b/solution.py
@@ -153,7 +153,9 @@
     ffn_width = w_gate.shape[1]
     joined = jnp.concatenate([w_gate, w_up], axis=1)
     partial_both = jnp.dot(normed_all, joined, preferred_element_type=jnp.float32)
-    summed = lax.psum(partial_both, "kvh")
+    summed = partial_both
+    for hop in (1, 2, 4):
+        summed = summed + lax.ppermute(summed, "kvh", [(dev, dev ^ hop) for dev in range(8)])
     hidden = (jax.nn.silu(summed[:, :ffn_width]) * summed[:, ffn_width:]).astype(jnp.bfloat16)
     lowered = lax.psum_scatter(
         jnp.dot(hidden, w_down, preferred_element_type=jnp.float32),

time: 342 us -> 316 us (0.924)
  waiting for transfers between devices: 203 us -> 170 us
  starting transfers between devices: 7.46 us -> 13.3 us
    psum x1 -> x0, waiting for transfers between devices: 62.3 us -> none  [per_device(): summed = lax.psum(partial_both, 'kvh')]
    ppermute x0 -> x3, waiting for transfers between devices: none -> 27 us  [per_device(): lax.ppermute(summed, 'kvh', [(dev, dev ^ hop) for dev in range(8)])]
    ppermute x0 -> x3, starting transfers between devices: none -> 5.86 us  [per_device(): lax.ppermute(summed, 'kvh', [(dev, dev ^ hop) for dev in range(8)])]
    unnamed x4 -> x3, waiting for transfers between devices: 84.2 us -> 84.6 us
  transfers between devices with their start and end apart: 4 -> 6, of which waited for: 3 -> 5; matrix products, arithmetic and copies ran while one was open for 10% -> 11% of each run, Pallas kernels for 0% -> 0%
where the time goes in v1:
time: 316 us; the launch traced here: 315 us
  waiting for transfers between devices  170 us (54%)
  blocking collectives  54.6 us (17%)
  local copies, waits for them, and re-layouts  26.6 us (8%)
  other arithmetic  21.8 us (7%)
  between operations  15 us (5%)
  starting transfers between devices  13.3 us (4%)
  matrix products  13.3 us (4%)
    unnamed x3, waiting for transfers between devices  84.6 us
    psum x1, waiting for transfers between devices, per_device(): attn_out = lax.psum(partial_out, 'kvh')  58.4 us
    all_gather x1, blocking collectives, per_device(): lax.all_gather(jnp.concatenate([normed_two, fresh_flat], axis=1), 'req',...  40.6 us
    ppermute x3, waiting for transfers between devices, per_device(): lax.ppermute(summed, 'kvh', [(dev, dev ^ hop) for dev in range(8)])  27 us
    select_n x2, other arithmetic, mask_blocks(): jnp.where(kept, blocks, jnp.where(placed, fresh[:, None, :, None, :], jnp...  15.3 us
    all_gather x1, blocking collectives, per_device(): full_states = lax.all_gather(states, 'kvh', axis=1, tiled=True)  14 us
    gather x3, local copies, waits for them, and re-layouts, per_device(): parcels = kv_pool[page_table[picked]]  9.99 us
    all_to_all x1, starting transfers between devices, per_device(): lax.all_to_all(parcels, 'req', split_axis=0, concat_axis=0, tiled=True)  7.34 us
  transfers between devices with their start and end apart: 6, of which 5 were waited for; matrix products, arithmetic and copies ran while one was open for 11% of the time, Pallas kernels for 0%

profile of v1, /device:TPU:0, one launch (start us, length us, event | category | flops | bytes accessed | tf_op | source)
XLA Modules:
  0.0 314.6 jit_solution(9594333005106487388)
XLA Ops:
  7.2 0.8 compare_select_fusion.4
  8.0 1.0 scatter_custom_fusion
  9.0 0.6 gather_fusion.3
  9.7 0.6 iota_reduce_fusion
  10.3 1.2 gather_fusion.4
  11.7 0.1 reshape.467
  11.8 8.7 %gather_fusion.5 = bf16[128,128,256]{2,1,0:T(8,128)(2,1)} fusion(bf16[64,128,256]{2,1,0:T(8,128)(2,1)} %bitcast.79, s32[1024]{0:T(1024)S(1)} %pad_clamp_fusion.1), kind=kCustom, calls=%fused_computation.5 | custom fusion | bytes 16777728 | tf_op jit(solution)/shard_map/gather | solution.py:106
  20.5 7.3 %all-to-all-start = ((bf16[16,8,1,128,256]{4,3,1,2,0:T(8,128)(2,1)}), bf16[16,8,1,128,256]{4,3,1,2,0:T(8,128)(2,1)}, u32[]{:S(2)}, u32[]{:S(2)}) async-start(bf16[16,8,1,128,256]{4,3,1,2,0:T(8,128)(2,1)} %bitcast.81), calls=%async_computation | async-start | bytes 16777216 | tf_op jit(solution)/shard_map/all_to_all | solution.py:107
  28.0 0.6 gather_fusion
  28.7 14.0 %all-gather = bf16[8,320,8]{1,2,0:T(8,128)(2,1)S(1)} all-gather(bf16[1,320,8]{1,2,0:T(8,128)(2,1)S(1)} %bitcast.84), channel_id=1, replica_groups=mesh['req'=16,'kvh'=8] {'kvh'}, dimensions={0}, use_global_device_ids=true | all-gather | bytes 46080 | tf_op jit(solution)/shard_map/all_gather | solution.py:110
  42.8 0.1 reshape.517
  42.9 0.1 fusion.18
  43.0 0.1 fusion.20
  43.1 2.3 multiply_reduce_fusion.1
  45.4 0.1 copy.33
  45.5 5.1 %gather_fusion.1 = bf16[64,128,256]{2,1,0:T(8,128)(2,1)} fusion(bf16[64,128,256]{2,1,0:T(8,128)(2,1)} %bitcast.80, s32[1024]{0:T(1024)S(1)} %pad_clamp_fusion.4), kind=kCustom, calls=%fused_computation.1 | custom fusion | bytes 8388864 | tf_op jit(solution)/shard_map/gather | solution.py:131
  50.6 0.2 fusion.9
  50.8 1.4 multiply_reduce_fusion.2
  52.3 0.1 fusion.37
  52.5 0.1 multiply_cosine_fusion.1
  52.7 0.1 broadcast_compare_fusion.1
  52.9 7.6 %select_select_fusion.1 = bf16[8,1,1024,256]{3,2,0,1:T(8,128)(2,1)} fusion(bf16[8,1,1024,256]{3,2,0,1:T(8,128)(2,1)} %bitcast.83, pred[8,1024]{1,0:T(8,128)(4,1)S(1)} %get-tuple-element.13, pred[8,1024]{1,0:T(8,128)(4,1)S(1)} %get-tuple-element.12, bf16[8,256]{1,0:T(8,128)(2,1)S(1)} %maximum_bitcast_fusion), kind=kLoop, calls=%fused_computation.11 | loop fusion | flops 4194304 | bytes 8409088 | tf_op jit(solution)/shard_map/jit(_where)/select_n | solution.py:45
  60.6 2.5 fusion.48
  63.1 2.0 fusion.8
  65.1 1.1 fusion.26
  66.3 58.4 %all-reduce.4.cloned.1.call-done = f32[8,2560]{1,0:T(8,128)} async-done(((f32[8,2560]{1,0:T(8,128)}), f32[8,2560]{1,0:T(8,128)}) %all-reduce.4.cloned.1.call-update) | async-done | bytes 81936 | tf_op jit(solution)/shard_map/psum | solution.py:137
  124.7 1.0 multiply_reduce_fusion
  125.9 0.5 copy-done.4
  126.4 40.6 %all_gather.7 = bf16[128,576]{1,0:T(8,128)(2,1)S(1)} all-gather(bf16[8,576]{1,0:T(8,128)(2,1)S(1)} %pad_maximum_fusion), channel_id=1, replica_groups=mesh['req'=16,'kvh'=8] {'req'}, dimensions={0}, use_global_device_ids=true | all-gather | bytes 156672 | tf_op jit(solution)/shard_map/all_gather | solution.py:148
  166.9 1.8 fusion.10
  168.8 0.1 collective-permute-start
  168.8 2.0 collective-permute-done
  171.0 2.0 collective-permute-start.1
  172.9 14.3 %collective-permute-done.1 = f32[128,1216]{0,1:T(8,128)S(1)} collective-permute-done((f32[128,1216]{0,1:T(8,128)S(1)}, f32[128,1216]{0,1:T(8,128)S(1)}, u32[]{:S(2)}, u32[]{:S(2)}) %collective-permute-start.1) | collective-permute-done | bytes 622624 | tf_op jit(solution)/shard_map/ppermute | solution.py:158
  187.3 3.8 %collective-permute-start.2 = (f32[128,1216]{0,1:T(8,128)S(1)}, f32[128,1216]{0,1:T(8,128)}, u32[]{:S(2)}, u32[]{:S(2)}) collective-permute-start(f32[128,1216]{0,1:T(8,128)S(1)} %add.202), channel_id=1, source_target_pairs={{0,4},{1,5},{2,6},{3,7},{4,0},{5,1},{6,2},{7,3},{8,12},{9,13},{10,... | collective-permute-start | bytes 1867784 | tf_op jit(solution)/shard_map/ppermute | solution.py:158
  191.1 0.1 compare_select_fusion.9
  191.2 0.6 gather_fusion.2
  191.9 0.1 lt.108
  192.0 0.6 dynamic-slice
  193.4 0.1 slice.63
  193.5 0.6 gather_fusion.7
  194.0 10.7 %collective-permute-done.2 = f32[128,1216]{0,1:T(8,128)} collective-permute-done((f32[128,1216]{0,1:T(8,128)S(1)}, f32[128,1216]{0,1:T(8,128)}, u32[]{:S(2)}, u32[]{:S(2)}) %collective-permute-start.2) | collective-permute-done | bytes 622624 | tf_op jit(solution)/shard_map/ppermute | solution.py:158
  204.7 1.2 add.203
  205.9 2.0 fusion.15
  207.9 84.6 %all-reduce.6.cloned.1.call-done = f32[128,320]{1,0:T(8,128)} async-done(((f32[128,320]{1,0:T(8,128)}), f32[128,320]{1,0:T(8,128)}) %all-reduce.6.cloned.1.call-update) | async-done | bytes 163856
  292.5 1.4 fusion.25
  293.9 6.2 %gather_fusion.6 = bf16[8,8,128,256]{3,2,1,0:T(8,128)(2,1)} fusion(bf16[16,8,128,256]{3,2,1,0:T(8,128)(2,1)} %bitcast.16, s32[1024]{0:T(1024)S(1)} %pad_clamp_fusion), kind=kCustom, calls=%fused_computation.6 | custom fusion | bytes 8388640 | tf_op jit(solution)/shard_map/gather | solution.py:167
  300.1 7.6 %select_select_fusion = bf16[64,1,128,256]{3,2,1,0:T(8,128)(2,1)} fusion(bf16[64,1,128,256]{3,2,1,0:T(8,128)(2,1)} %bitcast.82, pred[64,128]{1,0:T(8,128)(4,1)S(1)} %get-tuple-element.11, pred[64,128]{1,0:T(8,128)(4,1)S(1)} %get-tuple-element.10, bf16[64,256]{1,0:T(8,128)(2,1)S(1)} %broadcast_bitcast_fusion), kind=kLoop, calls=%fused_computation.10 | loop fusion | flops 4194304 | bytes 8437760 | tf_op jit(solution)/shard_map/jit(_where)/select_n | solution.py:45
  (69 shorter events, 1.4 us)
Async XLA Ops:
  7.2 57.9 %copy-start = (bf16[512,2560]{1,0:T(8,128)(2,1)S(1)}, bf16[512,2560]{1,0:T(8,128)(2,1)}, u32[]{:S(2)}) copy-start(bf16[512,2560]{1,0:T(8,128)(2,1)} %param.23) | copy-start | bytes 7864324
  20.5 7.4 %copy-start.2 = (s32[8,8]{1,0:T(8,128)S(1)}, s32[8,8]{1,0:T(8,128)}, u32[]{:S(2)}) copy-start(s32[8,8]{1,0:T(8,128)} %param.30) | copy-start | bytes 772
  20.5 7.5 %copy-start.10 = (bf16[128]{0:T(256)(128)(2,1)S(1)}, bf16[128]{0:T(256)(128)(2,1)}, u32[]{:S(2)}) copy-start(bf16[128]{0:T(256)(128)(2,1)} %param.21) | copy-start | bytes 772
  20.5 7.5 %copy-start.11 = (bf16[128]{0:T(256)(128)(2,1)S(1)}, bf16[128]{0:T(256)(128)(2,1)}, u32[]{:S(2)}) copy-start(bf16[128]{0:T(256)(128)(2,1)} %param.22) | copy-start | bytes 772
  20.5 7.5 %copy-start.1 = (s32[128]{0:T(128)S(1)}, s32[128]{0:T(128)}, u32[]{:S(2)}) copy-start(s32[128]{0:T(128)} %param.29) | copy-start | bytes 1540
  20.5 8.2 %copy-start.6 = (bf16[2560]{0:T(1024)(128)(2,1)S(1)}, bf16[2560]{0:T(1024)(128)(2,1)}, u32[]{:S(2)}) copy-start(bf16[2560]{0:T(1024)(128)(2,1)} %param.17) | copy-start | bytes 15364
  20.5 8.2 %copy-start.5 = (bf16[8,320]{1,0:T(8,128)(2,1)S(1)}, bf16[8,320]{1,0:T(8,128)(2,1)}, u32[]{:S(2)}) copy-start(bf16[8,320]{1,0:T(8,128)(2,1)} %param.16) | copy-start | bytes 15364
  20.5 273.4 %all-to-all-start = ((bf16[16,8,1,128,256]{4,3,1,2,0:T(8,128)(2,1)}), bf16[16,8,1,128,256]{4,3,1,2,0:T(8,128)(2,1)}, u32[]{:S(2)}, u32[]{:S(2)}) async-start(bf16[16,8,1,128,256]{4,3,1,2,0:T(8,128)(2,1)} %bitcast.81), calls=%async_computation | async-start | bytes 16777216 | tf_op jit(solution)/shard_map/all_to_all | solution.py:107
  27.8 96.8 %all-reduce.4.cloned.1.call-start = ((), (), s32[]{:S(2)}) async-start(), calls=%async_computation.1 | async-start | bytes 163840 | tf_op jit(solution)/shard_map/psum | solution.py:137
  45.5 5.1 %copy-start.3 = (bf16[2560,128]{1,0:T(8,128)(2,1)S(1)}, bf16[2560,128]{1,0:T(8,128)(2,1)}, u32[]{:S(2)}) copy-start(bf16[2560,128]{1,0:T(8,128)(2,1)} %param.20) | copy-start | bytes 1966084
  60.6 5.7 %copy-start.7 = (bf16[320]{0:T(512)(128)(2,1)S(1)}, bf16[320]{0:T(512)(128)(2,1)}, u32[]{:S(2)}) copy-start(bf16[320]{0:T(512)(128)(2,1)} %param.24) | copy-start | bytes 1924
  60.6 106.4 %copy-start.9 = (bf16[320,608]{1,0:T(8,128)(2,1)S(1)}, bf16[320,608]{1,0:T(8,128)(2,1)}, u32[]{:S(2)}) copy-start(bf16[320,608]{1,0:T(8,128)(2,1)} %param.26) | copy-start | bytes 1167364
  65.1 126.0 %copy-start.8 = (s32[128]{0:T(128)S(1)}, s32[128]{0:T(128)}, u32[]{:S(2)}) copy-start(s32[128]{0:T(128)} %param.31) | copy-start | bytes 1540
  65.1 126.9 %copy-start.12 = (u32[128]{0:T(128)S(1)}, u32[128]{0:T(128)}, u32[]{:S(2)}) copy-start(u32[128]{0:T(128)} %constant.91) | copy-start | bytes 1540
  66.2 226.3 %all-reduce.6.cloned.1.call-start = ((), (), s32[]{:S(2)}) async-start(), calls=%async_computation.2 | async-start | bytes 393216
  125.7 0.6 copy-start.4
  168.8 2.1 collective-permute-start
  171.0 16.3 %collective-permute-start.1 = (f32[128,1216]{0,1:T(8,128)S(1)}, f32[128,1216]{0,1:T(8,128)S(1)}, u32[]{:S(2)}, u32[]{:S(2)}) collective-permute-start(f32[128,1216]{0,1:T(8,128)S(1)} %add.201), channel_id=1, source_target_pairs={{0,2},{1,3},{2,0},{3,1},{4,6},{5,7},{6,4},{7,5},{8,10},{9,11},{10,... | collective-permute-start | bytes 1867784 | tf_op jit(solution)/shard_map/ppermute | solution.py:158
  187.3 17.4 %collective-permute-start.2 = (f32[128,1216]{0,1:T(8,128)S(1)}, f32[128,1216]{0,1:T(8,128)}, u32[]{:S(2)}, u32[]{:S(2)}) collective-permute-start(f32[128,1216]{0,1:T(8,128)S(1)} %add.202), channel_id=1, source_target_pairs={{0,4},{1,5},{2,6},{3,7},{4,0},{5,1},{6,2},{7,3},{8,12},{9,13},{10,... | collective-permute-start | bytes 1867784 | tf_op jit(solution)/shard_map/ppermute | solution.py:158
Sparse Core Ops, SparseCore 0:
  66.4 58.2 all-reduce.3
  208.0 84.4 all-reduce.5
